TPU v7x, 256 devices: a whole 4x4x8 slice. The times are simulated.
256 devices in a mesh: blk: 32 (over x, y, core), sub: 8 (over z).
Axes of the slice: x: 4, y: 4, z: 8, core: 2. Of those that a mesh axis runs over, the one named last changes fastest.
Arguments:
- block_vec: bfloat16 [64, 512, 512], P('blk', 'sub'), may hold values from -6 to 6
- left_factor: bfloat16 [8, 512, 512], replicated, may hold values from -0.25 to 0.25
- right_factor: bfloat16 [8, 512, 512], replicated, may hold values from -0.25 to 0.25
- pairs: int32 [32, 32, 2, 3], replicated, may hold values from 0 to 7, as said below
- pair_count: int32 [32, 32], replicated, may hold values from 1 to 2, as said below
- left_basis: bfloat16 [64, 512, 512], P('blk'), may hold values from -0.25 to 0.25
- left_dual: bfloat16 [64, 512, 512], P('blk'), may hold values from -0.25 to 0.25
- right_eigenvector_matrix: bfloat16 [64, 512, 512], P('blk'), may hold values from -0.25 to 0.25
- right_dual: bfloat16 [64, 512, 512], P('blk'), may hold values from -0.25 to 0.25
- left_rates: float32 [64, 512], P('blk', 'sub'), may hold values from 0.5 to 8
- right_rates: float32 [64, 512], P('blk'), may hold values from 0.5 to 8
Outputs:
- next_vec: float32 [64, 512, 512], P('blk', None, 'sub')
Inputs may be any that keep to these rules, and one draw needn't show every extreme that they name: `pairs`: entry [g, h, c, 0] is a source block index within group g, [g, h, c, 1] a target block index within group h (0 to 1), and [g, h, c, 2] a term index (0 to 7); where g equals h, source and target differ. For some target group h, pair_count[g, h] is 2 for every g.
All inputs are finite; a program needn't handle non-finite values.
Results may differ from a plain program's by a relative error of at most 0.023.
Values may be sent and summed in bfloat16 or wider, within the bound.
No kernel may reach another device: no remote copies, remote signals or barrier semaphores. Data moves between devices by JAX's collectives and lax.ppermute only.
A program may use at most 64 MiB of HBM per device.

v0:
```python
import jax
import jax.numpy as jnp
from jax import lax
from jax.sharding import PartitionSpec as P


def local(
    block_vec,
    left_factor,
    right_factor,
    pairs,
    pair_count,
    left_basis,
    left_dual,
    right_eigenvector_matrix,
    right_dual,
    left_rates,
    right_rates,
):
    owner = lax.axis_index("blk")
    groups = lax.axis_size("blk")
    local_blocks = block_vec.shape[0]
    row_count = block_vec.shape[1]
    width_two = block_vec.shape[2]
    slots_per = pairs.shape[2]
    term_total = left_factor.shape[0]
    all_count = groups * local_blocks
    incoming = lax.dynamic_index_in_dim(pairs, owner, 1, keepdims=False)
    counts = lax.dynamic_index_in_dim(pair_count, owner, 1, keepdims=False)
    live_mask = (jnp.arange(slots_per)[None, :] < counts[:, None]).astype(jnp.float32)
    target_term = incoming[..., 1] * term_total + incoming[..., 2]
    source = jnp.arange(groups, dtype=jnp.int32)[:, None] * local_blocks + incoming[..., 0]
    key_onehot = (
        target_term[..., None] == jnp.arange(local_blocks * term_total)[None, None, :]
    ).astype(jnp.float32) * live_mask[..., None]
    source_onehot = (source[..., None] == jnp.arange(all_count)[None, None, :]).astype(jnp.float32)
    weights = jnp.einsum("gqk,gqs->ks", key_onehot, source_onehot).astype(jnp.bfloat16)
    everything = lax.all_gather(block_vec, "blk", axis=0, tiled=True)
    pooled = jnp.einsum(
        "ks,srn->krn", weights, everything, preferred_element_type=jnp.float32
    ).astype(jnp.bfloat16)
    pooled = pooled.reshape(local_blocks, term_total, row_count, width_two)
    right_done = jnp.einsum(
        "ktrn,tmn->ktrm", pooled, right_factor, preferred_element_type=jnp.float32
    ).astype(jnp.bfloat16)
    right_cols = lax.all_to_all(right_done, "sub", split_axis=3, concat_axis=2, tiled=True)
    summed = jnp.einsum(
        "tab,ktbc->kac", left_factor, right_cols, preferred_element_type=jnp.float32
    ).astype(jnp.bfloat16)
    dual_cols = jnp.einsum(
        "jab,jbc->jac", left_dual, summed, preferred_element_type=jnp.float32
    ).astype(jnp.bfloat16)
    dual_rows = lax.all_to_all(dual_cols, "sub", split_axis=1, concat_axis=2, tiled=True)
    mixed = jnp.einsum("jrn,jmn->jrm", dual_rows, right_dual, preferred_element_type=jnp.float32)
    scaled = (mixed / (left_rates[:, :, None] + right_rates[:, None, :])).astype(jnp.bfloat16)
    basis_rows = jnp.einsum(
        "jrm,jkm->jrk", scaled, right_eigenvector_matrix, preferred_element_type=jnp.float32
    ).astype(jnp.bfloat16)
    basis_cols = lax.all_to_all(basis_rows, "sub", split_axis=2, concat_axis=1, tiled=True)
    return jnp.einsum("jab,jbc->jac", left_basis, basis_cols, preferred_element_type=jnp.float32)


def solution(mesh):
    placed = (
        P("blk", "sub", None),
        P(),
        P(),
        P(),
        P(),
        P("blk", None, None),
        P("blk", None, None),
        P("blk", None, None),
        P("blk", None, None),
        P("blk", "sub"),
        P("blk", None),
    )
    return jax.shard_map(
        local, mesh=mesh, in_specs=placed, out_specs=P("blk", None, "sub"), check_vma=False
    )
```

profile of v0, /device:TPU:2, one launch (start us, length us, event | category | flops | bytes accessed | tf_op | source)
XLA Modules:
  0.0 167.2 jit_solution(14784271772205998171)
XLA Ops:
  6.5 0.0 copy-start
  6.5 0.0 all-gather.2.cloned.1.call-start
  6.5 0.7 all-gather.2.cloned.1.call-update
  7.3 1.1 constant_dynamic-slice_fusion
  8.3 0.1 copy.25
  8.4 0.9 dynamic-slice_reduce_fusion
  9.4 54.3 %all-gather.2.cloned.1.call-done = bf16[64,64,512]{2,1,0:T(8,128)(2,1)} async-done(((bf16[2,64,512]{2,1,0:T(8,128)(2,1)}), bf16[64,64,512]{2,1,0:T(8,128)(2,1)}) %all-gather.2.cloned.1.call-update) | async-done | bytes 4194320 | tf_op jit(solution)/shard_map/all_gather | solution.py:38
  63.7 6.7 %fusion.15 = bf16[2,8,64,512]{3,1,0,2:T(8,128)(2,1)S(1)} fusion(bf16[64,64,512]{2,1,0:T(8,128)(2,1)} %all-gather.2.cloned.1.call-done, s32[32,2]{0,1:T(2,128)S(1)} %get-tuple-element.6, bf16[32,2]{0,1:T(2,128)(2,1)S(1)} %compare_convert_fusion, s32[32,2]{0,1:T(2,128)S(1)} %get-tuple-element.5), kind=kOutput, calls=%fused_computation.10 | convolution fusion | flops 67770368 | bytes 5243520 | tf_op jit(solution)/shard_map/ks,srn->krn/dot_general | solution.py:39
  70.4 4.8 %fusion.12 = bf16[2,8,64,512]{3,2,0,1:T(8,128)(2,1)} fusion(bf16[8,512,512]{2,1,0:T(8,128)(2,1)} %param.13, bf16[2,8,64,512]{3,1,0,2:T(8,128)(2,1)S(1)} %fusion.15), kind=kOutput, calls=%fused_computation.9 | convolution fusion | flops 537395200 | bytes 6291456 | tf_op jit(solution)/shard_map/ktrn,tmn->ktrm/dot_general | solution.py:43
  75.2 4.7 %copy.28 = bf16[2,8,64,512]{2,0,1,3:T(2,128)(2,1)S(1)} copy(bf16[2,8,64,512]{3,2,0,1:T(8,128)(2,1)} %fusion.12) | data formatting | bytes 2097152 | tf_op jit(solution)/shard_map/convert_element_type | solution.py:45
  80.0 2.7 %reshape.46 = bf16[8,2,32768]{2,1,0:T(2,128)(2,1)} reshape(bf16[512,8,2,64]{3,2,1,0:T(2,128)(2,1)S(1)} %bitcast.85) | data formatting | bytes 2097152
  82.6 36.3 %all_to_all.54 = bf16[8,2,32768]{2,1,0:T(2,128)(2,1)} all-to-all(bf16[8,2,32768]{2,1,0:T(2,128)(2,1)} %reshape.46), channel_id=1, replica_groups=mesh['blk'=32,'sub'=8] {'sub'}, dimensions={0} | all-to-all | bytes 2097152 | tf_op jit(solution)/shard_map/all_to_all | solution.py:46
  118.9 3.1 %reshape.47 = bf16[512,8,2,64]{3,2,1,0:T(2,128)(2,1)S(1)} reshape(bf16[8,2,32768]{2,1,0:T(2,128)(2,1)} %all_to_all.54) | data formatting | bytes 2097152
  122.0 2.7 %copy.47 = bf16[2,8,64,8,64]{2,3,4,1,0:T(8,128)(2,1)} copy(bf16[2,8,64,8,64]{2,0,1,4,3:T(2,128)(2,1)S(1)} %bitcast.86) | data formatting | bytes 2097152 | tf_op jit(solution)/shard_map/all_to_all | solution.py:46
  124.7 3.2 %all_to_all.42 = bf16[2,8,512,64]{2,3,1,0:T(8,128)(2,1)S(1)} reshape(bf16[2,8,8,64,64]{3,2,4,1,0:T(8,128)(2,1)} %bitcast.87) | data formatting | bytes 2097152 | tf_op jit(solution)/shard_map/all_to_all | solution.py:46
  127.9 0.0 copy-done
  127.9 0.0 copy-start.2
  127.9 0.0 copy-start.3
  127.9 4.0 %fusion.25 = bf16[2,512,64]{1,2,0:T(8,128)(2,1)S(1)} fusion(bf16[2,512,512]{2,1,0:T(8,128)(2,1)S(1)} %copy-done, bf16[2,8,512,64]{2,3,1,0:T(8,128)(2,1)S(1)} %all_to_all.42, bf16[8,512,512]{2,1,0:T(8,128)(2,1)} %param.12), kind=kOutput, calls=%fused_computation.18 | convolution fusion | flops 604110848 | bytes 6422528 | tf_op jit(solution)/shard_map/jab,jbc->jac/dot_general | solution.py:50
  131.9 0.0 copy-start.1
  131.9 0.2 copy.30
  132.1 0.2 reshape.48
  132.3 11.5 %all_to_all.55 = bf16[8,2,4096]{2,1,0:T(2,128)(2,1)S(1)} all-to-all(bf16[8,2,4096]{2,1,0:T(2,128)(2,1)S(1)} %reshape.48), channel_id=1, replica_groups=mesh['blk'=32,'sub'=8] {'sub'}, dimensions={0} | all-to-all | bytes 262144 | tf_op jit(solution)/shard_map/all_to_all | solution.py:53
  143.8 0.2 reshape.49
  144.0 0.2 copy.49
  144.2 0.2 all_to_all.46
  144.4 0.0 copy-done.2
  144.4 0.0 copy-done.3
  144.4 2.3 %convolution_convert_fusion = bf16[2,64,512]{2,1,0:T(8,128)(2,1)S(1)} fusion(bf16[2,512,512]{2,1,0:T(8,128)(2,1)} %param.18, bf16[2,64,512]{2,1,0:T(8,128)(2,1)S(1)} %all_to_all.46, bf16[2,512,512]{2,1,0:T(8,128)(2,1)} %param.19, f32[2,512]{1,0:T(2,128)S(1)} %copy-done.2, f32[2,64]{1,0:T(2,128)S(1)} %copy-done.3), kind=kOutput, calls=%fused_computation.15 | convolution fusion | flops 134479872 | bytes 2363904 | tf_op jit(solution)/shard_map/jrm,jkm->jrk/dot_general | solution.py:56
  146.7 0.2 copy.32
  146.9 0.2 reshape.50
  147.1 11.5 %all_to_all.56 = bf16[8,2,4096]{2,1,0:T(2,128)(2,1)S(1)} all-to-all(bf16[8,2,4096]{2,1,0:T(2,128)(2,1)S(1)} %reshape.50), channel_id=1, replica_groups=mesh['blk'=32,'sub'=8] {'sub'}, dimensions={0} | all-to-all | bytes 262144 | tf_op jit(solution)/shard_map/all_to_all | solution.py:59
  158.6 0.2 reshape.51
  158.8 0.2 copy.48
  159.0 0.2 all_to_all.50
  159.2 0.0 copy-done.1
  159.2 1.1 convolution_bitcast_fusion
  (3 shorter events, 0.0 us)
Async XLA Ops:
  6.5 121.3 %copy-start = (bf16[2,512,512]{2,1,0:T(8,128)(2,1)S(1)}, bf16[2,512,512]{2,1,0:T(8,128)(2,1)}, u32[]{:S(2)}) copy-start(bf16[2,512,512]{2,1,0:T(8,128)(2,1)} %param.17) | copy-start | bytes 3145732
  6.5 57.1 %all-gather.2.cloned.1.call-start = ((), (), s32[]{:S(2)}) async-start(), calls=%async_computation.3 | async-start | bytes 4325376 | tf_op jit(solution)/shard_map/all_gather | solution.py:38
  127.9 16.5 %copy-start.2 = (f32[2,512]{1,0:T(2,128)S(1)}, f32[2,512]{1,0:T(2,128)}, u32[]{:S(2)}) copy-start(f32[2,512]{1,0:T(2,128)} %param.21) | copy-start | bytes 12292
  127.9 16.5 %copy-start.3 = (f32[2,64]{1,0:T(2,128)S(1)}, f32[2,64]{1,0:T(2,128)}, u32[]{:S(2)}) copy-start(f32[2,64]{1,0:T(2,128)} %param.20) | copy-start | bytes 1540
  131.9 27.3 %copy-start.1 = (bf16[2,512,512]{2,1,0:T(8,128)(2,1)S(1)}, bf16[2,512,512]{2,1,0:T(8,128)(2,1)}, u32[]{:S(2)}) copy-start(bf16[2,512,512]{2,1,0:T(8,128)(2,1)} %param.16) | copy-start | bytes 3145732
Sparse Core Ops, SparseCore 0:
  9.9 53.7 all-gather.1
where the time goes:
time: 168 us; the launch traced here: 167 us
  blocking collectives  59.2 us (35%)
  waiting for transfers between devices  55 us (33%)
  local copies, waits for them, and re-layouts  20.5 us (12%)
  matrix products  19 us (11%)
  between operations  13.6 us (8%)
    all_gather x1, waiting for transfers between devices, local(): everything = lax.all_gather(block_vec, 'blk', axis=0, tiled=True)  54.3 us
    all_to_all x1, blocking collectives, local(): lax.all_to_all(right_done, 'sub', split_axis=3, concat_axis=2, tiled=True)  36.3 us
    all_to_all x1, blocking collectives, local(): lax.all_to_all(dual_cols, 'sub', split_axis=1, concat_axis=2, tiled=True)  11.5 us
    all_to_all x1, blocking collectives, local(): lax.all_to_all(basis_rows, 'sub', split_axis=2, concat_axis=1, tiled=True)  11.5 us
    dot_general x1, matrix products, local(): jnp.einsum('ks,srn->krn', weights, everything, preferred_element_type=jnp...  6.75 us
    unnamed x14, local copies, waits for them, and re-layouts  6.67 us
    all_to_all x2, local copies, waits for them, and re-layouts, local(): lax.all_to_all(right_done, 'sub', split_axis=3, concat_axis=2, tiled=True)  5.88 us
    dot_general x1, matrix products, local(): jnp.einsum('ktrn,tmn->ktrm', pooled, right_factor, preferred_element_type...  4.8 us
  transfers between devices with their start and end apart: 1, of which 1 were waited for; matrix products, arithmetic and copies ran while one was open for 1% of the time, Pallas kernels for 0%

commit v1 on v0

--- a/solution.py
+++ b/solution.py
@@ -35,7 +35,8 @@
     ).astype(jnp.float32) * live_mask[..., None]
     source_onehot = (source[..., None] == jnp.arange(all_count)[None, None, :]).astype(jnp.float32)
     weights = jnp.einsum("gqk,gqs->ks", key_onehot, source_onehot).astype(jnp.bfloat16)
-    everything = lax.all_gather(block_vec, "blk", axis=0, tiled=True)
+    stack = jnp.stack([block_vec] * lax.axis_size("blk"))
+    everything = jnp.concatenate(lax.all_to_all(stack, "blk", 0, 0), axis=0)
     pooled = jnp.einsum(
         "ks,srn->krn", weights, everything, preferred_element_type=jnp.float32
     ).astype(jnp.bfloat16)

time: 168 us -> 180 us (1.071)
  the two profiles are of different devices: /device:TPU:2 before, /device:TPU:8 now
where the time goes in v1:
time: 180 us; the launch traced here: 179 us
  blocking collectives  60 us (33%)
  waiting for transfers between devices  54 us (30%)
  local copies, waits for them, and re-layouts  41.7 us (23%)
  matrix products  15.3 us (8%)
  starting transfers between devices  7.72 us (4%)
    all_to_all x1, waiting for transfers between devices, local(): everything = jnp.concatenate(lax.all_to_all(stack, 'blk', 0, 0), axis=0)  54 us
    all_to_all x1, blocking collectives, local(): lax.all_to_all(right_done, 'sub', split_axis=3, concat_axis=2, tiled=True)  37.1 us
    all_to_all x1, blocking collectives, local(): lax.all_to_all(dual_cols, 'sub', split_axis=1, concat_axis=2, tiled=True)  11.5 us
    all_to_all x1, blocking collectives, local(): lax.all_to_all(basis_rows, 'sub', split_axis=2, concat_axis=1, tiled=True)  11.5 us
    all_to_all x1, local copies, waits for them, and re-layouts, local(): everything = jnp.concatenate(lax.all_to_all(stack, 'blk', 0, 0), axis=0)  8.76 us
    unnamed x19, local copies, waits for them, and re-layouts  7.81 us
    all_to_all x1, starting transfers between devices, local(): everything = jnp.concatenate(lax.all_to_all(stack, 'blk', 0, 0), axis=0)  7.72 us
    reshape x1, local copies, waits for them, and re-layouts, local(): everything = jnp.concatenate(lax.all_to_all(stack, 'blk', 0, 0), axis=0)  7.18 us
  transfers between devices with their start and end apart: 1, of which 1 were waited for; matrix products, arithmetic and copies ran while one was open for 0% of the time, Pallas kernels for 0%

profile of v1, /device:TPU:8, one launch (start us, length us, event | category | flops | bytes accessed | tf_op | source)
XLA Modules:
  0.0 178.9 jit_solution(3544204100927510159)
XLA Ops:
  0.0 0.0 copy-start
  0.0 1.1 copy.26
  1.1 5.7 %stack.2 = bf16[32,2,64,512]{3,1,2,0:T(2,128)(2,1)} broadcast(bf16[2,64,512]{2,0,1:T(2,128)(2,1)S(1)} %copy.26), dimensions={1,2,3} | broadcast | bytes 4325376 | tf_op jit(solution)/shard_map/stack | solution.py:38
  6.9 0.0 copy-start.2
  6.9 0.0 copy-start.3
  6.9 7.7 %all-to-all-start = ((bf16[32,2,64,512]{3,1,2,0:T(2,128)(2,1)}), bf16[32,2,64,512]{3,1,2,0:T(2,128)(2,1)}, u32[]{:S(2)}, u32[]{:S(2)}) async-start(bf16[32,2,64,512]{3,1,2,0:T(2,128)(2,1)} %stack.2), calls=%async_computation | async-start | bytes 8388608 | tf_op jit(solution)/shard_map/all_to_all | solution.py:39
  14.6 0.0 copy-done.2
  14.6 0.2 constant_dynamic-slice_fusion
  14.8 0.1 copy.25
  14.9 0.0 copy-done.3
  14.9 0.2 dynamic-slice_reduce_fusion
  15.1 54.0 %all-to-all-done = bf16[32,2,64,512]{3,1,2,0:T(2,128)(2,1)} async-done(((bf16[32,2,64,512]{3,1,2,0:T(2,128)(2,1)}), bf16[32,2,64,512]{3,1,2,0:T(2,128)(2,1)}, u32[]{:S(2)}, u32[]{:S(2)}) %all-to-all-start) | async-done | bytes 4194336 | tf_op jit(solution)/shard_map/all_to_all | solution.py:39
  69.2 8.8 %copy.27 = bf16[32,2,64,512]{3,1,0,2:T(2,128)(2,1)} copy(bf16[32,2,64,512]{3,1,2,0:T(2,128)(2,1)} %all-to-all-done) | data formatting | bytes 8388608 | tf_op jit(solution)/shard_map/all_to_all | solution.py:39
  77.9 7.2 %reshape.44 = bf16[64,64,512]{2,0,1:T(8,128)(2,1)} reshape(bf16[32,2,64,512]{3,1,0,2:T(2,128)(2,1)} %copy.27) | data formatting | bytes 8388608 | tf_op jit(solution)/shard_map/reshape | solution.py:39
  85.1 3.0 %fusion.7 = bf16[2,8,64,512]{3,1,0,2:T(8,128)(2,1)S(1)} fusion(bf16[64,64,512]{2,0,1:T(8,128)(2,1)} %reshape.44, s32[32,2]{0,1:T(2,128)S(1)} %get-tuple-element.6, bf16[32,2]{0,1:T(2,128)(2,1)S(1)} %compare_convert_fusion, s32[32,2]{0,1:T(2,128)S(1)} %get-tuple-element.5), kind=kOutput, calls=%fused_computation.7 | convolution fusion | flops 67770368 | bytes 5243520 | tf_op jit(solution)/shard_map/ks,srn->krn/dot_general | solution.py:40
  88.1 4.8 %fusion.8 = bf16[2,8,64,512]{3,2,0,1:T(8,128)(2,1)} fusion(bf16[8,512,512]{2,1,0:T(8,128)(2,1)} %param.13, bf16[2,8,64,512]{3,1,0,2:T(8,128)(2,1)S(1)} %fusion.7), kind=kOutput, calls=%fused_computation.8 | convolution fusion | flops 537395200 | bytes 6291456 | tf_op jit(solution)/shard_map/ktrn,tmn->ktrm/dot_general | solution.py:44
  92.9 4.7 %copy.29 = bf16[2,8,64,512]{2,0,1,3:T(2,128)(2,1)S(1)} copy(bf16[2,8,64,512]{3,2,0,1:T(8,128)(2,1)} %fusion.8) | data formatting | bytes 2097152 | tf_op jit(solution)/shard_map/convert_element_type | solution.py:46
  97.7 2.7 %reshape.52 = bf16[8,2,32768]{2,1,0:T(2,128)(2,1)} reshape(bf16[512,8,2,64]{3,2,1,0:T(2,128)(2,1)S(1)} %bitcast.88) | data formatting | bytes 2097152
  100.3 37.1 %all_to_all.59 = bf16[8,2,32768]{2,1,0:T(2,128)(2,1)} all-to-all(bf16[8,2,32768]{2,1,0:T(2,128)(2,1)} %reshape.52), channel_id=1, replica_groups=mesh['blk'=32,'sub'=8] {'sub'}, dimensions={0} | all-to-all | bytes 2097152 | tf_op jit(solution)/shard_map/all_to_all | solution.py:47
  137.4 3.1 %reshape.53 = bf16[512,8,2,64]{3,2,1,0:T(2,128)(2,1)S(1)} reshape(bf16[8,2,32768]{2,1,0:T(2,128)(2,1)} %all_to_all.59) | data formatting | bytes 2097152
  140.5 2.7 %copy.42 = bf16[2,8,64,8,64]{2,3,4,1,0:T(8,128)(2,1)} copy(bf16[2,8,64,8,64]{2,0,1,4,3:T(2,128)(2,1)S(1)} %bitcast.89) | data formatting | bytes 2097152 | tf_op jit(solution)/shard_map/all_to_all | solution.py:47
  143.2 3.2 %all_to_all.46 = bf16[2,8,512,64]{2,3,1,0:T(8,128)(2,1)S(1)} reshape(bf16[2,8,8,64,64]{3,2,4,1,0:T(8,128)(2,1)} %bitcast.90) | data formatting | bytes 2097152 | tf_op jit(solution)/shard_map/all_to_all | solution.py:47
  146.4 0.0 copy-done
  146.5 0.0 copy-start.4
  146.5 0.0 copy-start.5
  146.5 4.0 %fusion.18 = bf16[2,512,64]{1,2,0:T(8,128)(2,1)S(1)} fusion(bf16[2,512,512]{2,1,0:T(8,128)(2,1)S(1)} %copy-done, bf16[2,8,512,64]{2,3,1,0:T(8,128)(2,1)S(1)} %all_to_all.46, bf16[8,512,512]{2,1,0:T(8,128)(2,1)} %param.12), kind=kOutput, calls=%fused_computation.16 | convolution fusion | flops 604110848 | bytes 6422528 | tf_op jit(solution)/shard_map/jab,jbc->jac/dot_general | solution.py:51
  150.5 0.0 copy-start.1
  150.5 0.2 copy.31
  150.6 0.2 reshape.54
  150.9 11.5 %all_to_all.60 = bf16[8,2,4096]{2,1,0:T(2,128)(2,1)S(1)} all-to-all(bf16[8,2,4096]{2,1,0:T(2,128)(2,1)S(1)} %reshape.54), channel_id=1, replica_groups=mesh['blk'=32,'sub'=8] {'sub'}, dimensions={0} | all-to-all | bytes 262144 | tf_op jit(solution)/shard_map/all_to_all | solution.py:54
  162.4 0.2 reshape.55
  162.6 0.2 copy.44
  162.8 0.2 all_to_all.50
  163.0 0.0 copy-done.4
  163.0 0.0 copy-done.5
  163.0 2.3 %convolution_convert_fusion.1 = bf16[2,64,512]{2,1,0:T(8,128)(2,1)S(1)} fusion(bf16[2,512,512]{2,1,0:T(8,128)(2,1)} %param.18, bf16[2,64,512]{2,1,0:T(8,128)(2,1)S(1)} %all_to_all.50, bf16[2,512,512]{2,1,0:T(8,128)(2,1)} %param.19, f32[2,512]{1,0:T(2,128)S(1)} %copy-done.4, f32[2,64]{1,0:T(2,128)S(1)} %copy-done.5), kind=kOutput, calls=%fused_computation.13 | convolution fusion | flops 134479872 | bytes 2363904 | tf_op jit(solution)/shard_map/jrm,jkm->jrk/dot_general | solution.py:57
  165.3 0.2 copy.33
  165.5 0.2 reshape.56
  165.7 11.5 %all_to_all.61 = bf16[8,2,4096]{2,1,0:T(2,128)(2,1)S(1)} all-to-all(bf16[8,2,4096]{2,1,0:T(2,128)(2,1)S(1)} %reshape.56), channel_id=1, replica_groups=mesh['blk'=32,'sub'=8] {'sub'}, dimensions={0} | all-to-all | bytes 262144 | tf_op jit(solution)/shard_map/all_to_all | solution.py:60
  177.2 0.2 reshape.57
  177.4 0.2 copy.43
  177.6 0.2 all_to_all.54
  177.8 0.0 copy-done.1
  177.8 1.1 convolution_bitcast_fusion
  (3 shorter events, 0.0 us)
Async XLA Ops:
  0.0 146.4 %copy-start = (bf16[2,512,512]{2,1,0:T(8,128)(2,1)S(1)}, bf16[2,512,512]{2,1,0:T(8,128)(2,1)}, u32[]{:S(2)}) copy-start(bf16[2,512,512]{2,1,0:T(8,128)(2,1)} %param.17) | copy-start | bytes 3145732
  6.9 7.7 %copy-start.2 = (s32[32,32,2,3]{1,2,3,0:T(2,128)S(1)}, s32[32,32,2,3]{1,2,3,0:T(2,128)}, u32[]{:S(2)}) copy-start(s32[32,32,2,3]{1,2,3,0:T(2,128)} %param.14) | copy-start | bytes 73732
  6.9 8.0 %copy-start.3 = (s32[32,32]{1,0:T(8,128)S(1)}, s32[32,32]{1,0:T(8,128)}, u32[]{:S(2)}) copy-start(s32[32,32]{1,0:T(8,128)} %param.15) | copy-start | bytes 12292
  6.9 62.3 %all-to-all-start = ((bf16[32,2,64,512]{3,1,2,0:T(2,128)(2,1)}), bf16[32,2,64,512]{3,1,2,0:T(2,128)(2,1)}, u32[]{:S(2)}, u32[]{:S(2)}) async-start(bf16[32,2,64,512]{3,1,2,0:T(2,128)(2,1)} %stack.2), calls=%async_computation | async-start | bytes 8388608 | tf_op jit(solution)/shard_map/all_to_all | solution.py:39
  146.5 16.5 %copy-start.4 = (f32[2,512]{1,0:T(2,128)S(1)}, f32[2,512]{1,0:T(2,128)}, u32[]{:S(2)}) copy-start(f32[2,512]{1,0:T(2,128)} %param.21) | copy-start | bytes 12292
  146.5 16.5 %copy-start.5 = (f32[2,64]{1,0:T(2,128)S(1)}, f32[2,64]{1,0:T(2,128)}, u32[]{:S(2)}) copy-start(f32[2,64]{1,0:T(2,128)} %param.20) | copy-start | bytes 1540
  150.5 27.3 %copy-start.1 = (bf16[2,512,512]{2,1,0:T(8,128)(2,1)S(1)}, bf16[2,512,512]{2,1,0:T(8,128)(2,1)}, u32[]{:S(2)}) copy-start(bf16[2,512,512]{2,1,0:T(8,128)(2,1)} %param.16) | copy-start | bytes 3145732
